TPU v7x, 256 devices: a whole 4x4x8 slice. The times are simulated.
256 devices in a mesh: ctx: 64 (over y, z_lo, x), tp: 4 (over z_hi, core).
Axes of the slice: x: 4, y: 4, z: 8 (z_hi: 2, z_lo: 4; z = z_hi * 4 + z_lo), core: 2. Of those that a mesh axis runs over, the one named last changes fastest.
Arguments:
- activations: bfloat16 [40960, 4096], P('ctx', 'tp'), may hold values from -6 to 6
- group_counts: int32 [64], replicated, may hold values from 1 to 5, as said below
- genome_starts: int32 [32], replicated, may hold values from 0 to 24448, as said below
- in_weight: bfloat16 [4096, 3, 2048], P('ctx', None, 'tp'), may hold values from -0.09375 to 0.09375
- short_taps: float32 [7, 3, 2048], P(None, None, 'tp'), may hold values from -2 to 2
- long_taps: float32 [128, 2048], P(None, 'tp'), may hold values from -0.5 to 0.5
- out_weight: bfloat16 [2048, 4096], P('tp', 'ctx'), may hold values from -0.125 to 0.125
Outputs:
- block_out: bfloat16 [40960, 4096], P('ctx', 'tp')
Inputs may be any that keep to these rules, and one draw needn't show every extreme that they name: Every device holds 1 or more blocks; group_counts[2k] + group_counts[2k+1] = 6 for every k. `genome_starts`: strictly increasing; the first entry is 0 and the last is exactly 24448.
All inputs are finite; a program needn't handle non-finite values.
Results may differ from a plain program's by a relative error of at most 0.012.
Values may be sent and summed in bfloat16 or wider, within the bound.
No kernel may reach another device: no remote copies, remote signals or barrier semaphores. Data moves between devices by JAX's collectives and lax.ppermute only.
A program may use at most 128 MiB of HBM per device.

v0:
```python
import jax
import jax.numpy as jnp
from jax import lax
from jax.sharding import PartitionSpec as P

GROUP = 128


def passed_along(shard, axis, by):
    peers = lax.axis_size(axis)
    pairs = [(i, i + by) for i in range(peers) if 0 <= i + by < peers]
    return lax.ppermute(shard, axis, pairs)


def genome_start(positions, genome_starts):
    above = genome_starts[None, :] <= positions[:, None]
    return jnp.max(jnp.where(above, genome_starts[None, :], 0), axis=1)


def causal_taps(padded, taps, positions, gstart, width):
    count = positions.shape[0]
    shape = (count,) + (1,) * (padded.ndim - 1)
    summed = jnp.zeros((count,) + padded.shape[1:], jnp.float32)
    for j in range(width):
        in_genome = (positions - j >= gstart).reshape(shape)
        window = padded[width - 1 - j : width - 1 - j + count]
        summed = summed + jnp.where(in_genome, window * taps[j], jnp.float32(0.0))
    return summed


def body(activations, group_counts, genome_starts, in_weight, short_taps, long_taps, out_weight):
    ctx_size = lax.axis_size("ctx")
    my_index = lax.axis_index("ctx")
    own_rows = activations.shape[0]
    device_ids = jnp.arange(ctx_size, dtype=jnp.int32)
    own_count = jnp.sum(jnp.where(device_ids == my_index, group_counts, 0))
    offset = jnp.sum(jnp.where(device_ids < my_index, group_counts, 0))
    row_ids = jnp.arange(own_rows, dtype=jnp.int32)
    positions = offset * GROUP + row_ids
    tail_end = own_count * GROUP

    def last_rows(source, count):
        return lax.dynamic_slice_in_dim(source, tail_end - count, count, 0)

    gstart = genome_start(positions, genome_starts)
    all_feats = lax.all_gather(activations, "tp", axis=1, tiled=True)
    widened = all_feats.astype(jnp.float32)
    normed = (
        widened * lax.rsqrt(jnp.mean(widened * widened, axis=1, keepdims=True) + 1e-06)
    ).astype(jnp.bfloat16)
    row_count = normed.shape[0]
    branches = in_weight.shape[1]
    chans = in_weight.shape[2]
    local_in = in_weight.reshape(in_weight.shape[0], branches * chans)
    both = jnp.concatenate([local_in, out_weight.T], axis=1)
    both_rows = lax.all_gather(both, "ctx", axis=0, tiled=True)
    flat = both_rows[:, : branches * chans]
    out_rows = both_rows[:, branches * chans :]
    summed = jnp.dot(normed, flat, preferred_element_type=jnp.float32)
    projected = summed.astype(jnp.bfloat16).reshape(row_count, branches, chans)
    rim_short = passed_along(last_rows(projected, 6), "ctx", 1)
    feat = causal_taps(
        jnp.concatenate([rim_short, projected], axis=0).astype(jnp.float32),
        short_taps,
        positions,
        gstart,
        7,
    )
    mixed = (feat[:, 1] * feat[:, 2]).astype(jnp.bfloat16)
    rim_long = passed_along(last_rows(mixed, 127), "ctx", 1)
    filtered = causal_taps(
        jnp.concatenate([rim_long, mixed], axis=0).astype(jnp.float32),
        long_taps,
        positions,
        gstart,
        128,
    )
    gated = (feat[:, 0] * filtered).astype(jnp.bfloat16)
    partial_out = lax.dot_general(
        gated, out_rows, (((1,), (1,)), ((), ())), preferred_element_type=jnp.float32
    )
    branch_out = lax.psum_scatter(
        partial_out.astype(jnp.bfloat16), "tp", scatter_dimension=1, tiled=True
    ).astype(jnp.float32)
    result = (activations.astype(jnp.float32) + branch_out).astype(jnp.bfloat16)
    slot_ids = jnp.arange(own_rows, dtype=jnp.int32)
    live_rows = (slot_ids < own_count * GROUP)[:, None]
    return jnp.where(live_rows, result, jnp.zeros_like(result))


def solution(mesh):
    placed = (
        P("ctx", "tp"),
        P(),
        P(),
        P("ctx", None, "tp"),
        P(None, None, "tp"),
        P(None, "tp"),
        P("tp", "ctx"),
    )
    return jax.shard_map(
        body, mesh=mesh, in_specs=placed, out_specs=P("ctx", "tp"), check_vma=False
    )
```

profile of v0, /device:TPU:1, one launch (start us, length us, event | category | flops | bytes accessed | tf_op | source)
XLA Modules:
  0.0 681.4 jit_solution(17413484477117585637)
XLA Ops:
  6.6 0.0 all-gather.3.cloned.1.call-start
  6.6 0.7 all-gather.3.cloned.1.call-update
  7.3 0.0 all-gather.5.cloned.1.call-start
  7.3 0.1 copy-done.2
  7.5 0.7 pad_maximum_fusion
  8.2 0.0 all-gather.5.cloned.1.call-update
  8.2 0.0 reduce-scatter.2.cloned.1.call-start
  8.3 0.7 fusion.287
  10.4 0.1 select_reduce_fusion
  10.9 1.3 add_compare_fusion.95
  12.2 79.5 %all-gather.3.cloned.1.call-done = bf16[640,4096]{1,0:T(8,128)(2,1)} async-done(((bf16[640,1024]{1,0:T(8,128)(2,1)}), bf16[640,4096]{1,0:T(8,128)(2,1)}) %all-gather.3.cloned.1.call-update) | async-done | bytes 5242896 | tf_op jit(solution)/shard_map/all_gather | solution.py:46
  91.6 3.6 fusion.2
  95.2 329.4 %all-gather.5.cloned.1.call-done = bf16[4096,2048]{1,0:T(8,128)(2,1)} async-done(((bf16[64,2048]{1,0:T(8,128)(2,1)}), bf16[4096,2048]{1,0:T(8,128)(2,1)}) %all-gather.5.cloned.1.call-update) | async-done | bytes 16777232 | tf_op jit(solution)/shard_map/all_gather | solution.py:56
  424.6 13.9 %fusion.20 = bf16[640,1536]{1,0:T(8,128)(2,1)} fusion(bf16[4096,2048]{1,0:T(8,128)(2,1)} %all-gather.5.cloned.1.call-done, bf16[640,4096]{1,0:T(8,128)(2,1)} %all-gather.3.cloned.1.call-done, f32[640]{0:T(1024)S(1)} %add_rsqrt_fusion), kind=kOutput, calls=%fused_computation.29 | convolution fusion | flops 8061911040 | bytes 19794432 | tf_op jit(solution)/shard_map/dot_general | solution.py:59
  438.5 2.8 copy.16
  441.3 0.2 constant_dynamic-slice_fusion
  441.4 2.1 collective-permute-start
  443.6 6.7 collective-permute-done
  450.3 1.0 maximum_convert_fusion
  451.4 8.1 %fusion.8 = f32[640,3,512]{0,2,1:T(8,128)S(1)} fusion(f32[646,3,512]{0,2,1:T(8,128)S(1)} %maximum_convert_fusion, f32[3,512]{1,0:T(4,128)S(1)} %get-tuple-element.270, f32[3,512]{1,0:T(4,128)S(1)} %get-tuple-element.271, f32[3,512]{1,0:T(4,128)S(1)} %get-tuple-element.272, f32[3,512]{1,0:T(4,128)S(1)} %get-tuple-element.273, ...), kind=kLoop, calls=%fused_computation.11 | loop fusion | flops 19660800 | bytes 31504768 | tf_op jit(solution)/shard_map/add | solution.py:27
  459.4 0.1 fusion.283
  459.6 0.1 dynamic-slice_bitcast_fusion
  459.7 4.4 collective-permute-start.1
  464.1 0.1 fusion.297
  464.2 1.6 collective-permute-done.1
  465.8 0.4 maximum_convert_fusion.1
  466.6 15.7 %fusion.221 = f32[640,512]{0,1:T(8,128)S(1)} fusion(f32[767,512]{0,1:T(8,128)S(1)} %maximum_convert_fusion.1, f32[512]{0:T(512)S(1)} %bitcast.198, f32[512]{0:T(512)S(1)} %bitcast.180, f32[512]{0:T(512)S(1)} %bitcast.181, f32[512]{0:T(512)S(1)} %bitcast.182, f32[512]{0:T(512)S(1)} %bitcast.183, f32[512]{0:T(512)S(1)} %bitcast.184, f32[512]{0:T(512)S(1)} %bitcast.185, ...), kind=kLoop, calls=%fused_computation.325 | loop fusion | flops 31129600 | bytes 43339776 | tf_op jit(solution)/shard_map/add | solution.py:27
  482.8 47.7 %fusion.304 = bf16[640,512]{0,1:T(8,128)(2,1)S(1)} fusion(f32[767,512]{0,1:T(8,128)S(1)} %maximum_convert_fusion.1, f32[640,512]{0,1:T(8,128)S(1)} %fusion.221, f32[512]{0:T(512)S(1)} %bitcast.199, f32[512]{0:T(512)S(1)} %bitcast.200, f32[512]{0:T(512)S(1)} %bitcast.239, f32[512]{0:T(512)S(1)} %bitcast.240, f32[512]{0:T(512)S(1)} %bitcast.241, ...), kind=kLoop, calls=%fused_computation.37.clone.clone.2 | loop fusion | flops 95027200 | bytes 129363968 | tf_op jit(solution)/shard_map/dot_general | solution.py:79
  530.5 7.5 %convolution_convert_fusion = bf16[640,4096]{1,0:T(8,128)(2,1)} fusion(bf16[4096,2048]{1,0:T(8,128)(2,1)} %all-gather.5.cloned.1.call-done, bf16[640,512]{0,1:T(8,128)(2,1)S(1)} %fusion.304), kind=kOutput, calls=%fused_computation.6 | convolution fusion | flops 2686976000 | bytes 10092544 | tf_op jit(solution)/shard_map/dot_general | solution.py:79
  538.0 0.0 reduce-scatter.2.cloned.1.call-update
  538.0 134.1 %reduce-scatter.2.cloned.1.call-done = bf16[640,1024]{1,0:T(8,128)(2,1)} async-done(((bf16[640,4096]{1,0:T(8,128)(2,1)}), bf16[640,1024]{1,0:T(8,128)(2,1)}) %reduce-scatter.2.cloned.1.call-update) | async-done | bytes 1310736 | tf_op jit(solution)/shard_map/reduce_scatter | solution.py:82
  672.1 2.8 fusion.25
  (109 shorter events, 0.5 us)
Async XLA Ops:
  6.6 85.1 %all-gather.3.cloned.1.call-start = ((), (), s32[]{:S(2)}) async-start(), calls=%async_computation.1 | async-start | bytes 6553600 | tf_op jit(solution)/shard_map/all_gather | solution.py:46
  7.3 417.3 %all-gather.5.cloned.1.call-start = ((), (), s32[]{:S(2)}) async-start(), calls=%async_computation.2 | async-start | bytes 17039360 | tf_op jit(solution)/shard_map/all_gather | solution.py:56
  8.2 663.8 %reduce-scatter.2.cloned.1.call-start = ((), (), s32[]{:S(2)}) async-start(), calls=%async_computation.3 | async-start | bytes 6553600 | tf_op jit(solution)/shard_map/reduce_scatter | solution.py:82
  441.4 8.9 %collective-permute-start = (bf16[6,3,512]{0,2,1:T(8,128)(2,1)S(1)}, bf16[6,3,512]{0,2,1:T(8,128)(2,1)S(1)}, u32[]{:S(2)}, u32[]{:S(2)}) collective-permute-start(bf16[6,3,512]{0,2,1:T(8,128)(2,1)S(1)} %constant_dynamic-slice_fusion), channel_id=1, source_target_pairs={{0,4},{4,8},{8,12},{12,16},{16,20},{20,24},{24,28},{28,32},{32,36}... | collective-permute-start | bytes 55304 | tf_op jit(solution)/shard_map/ppermute | solution.py:12
  459.7 6.1 collective-permute-start.1
  466.2 16.1 %copy-start.5 = (pred[640]{0:T(1024)(128)(4,1)S(1)}, pred[640]{0:T(1024)(128)(4,1)}, u32[]{:S(2)}) copy-start(pred[640]{0:T(1024)(128)(4,1)} %get-tuple-element.160) | copy-start | bytes 1924
  466.2 16.1 %copy-start.6 = (pred[640]{0:T(1024)(128)(4,1)S(1)}, pred[640]{0:T(1024)(128)(4,1)}, u32[]{:S(2)}) copy-start(pred[640]{0:T(1024)(128)(4,1)} %get-tuple-element.161) | copy-start | bytes 1924
  466.2 16.1 %copy-start.7 = (pred[640]{0:T(1024)(128)(4,1)S(1)}, pred[640]{0:T(1024)(128)(4,1)}, u32[]{:S(2)}) copy-start(pred[640]{0:T(1024)(128)(4,1)} %get-tuple-element.162) | copy-start | bytes 1924
  466.2 16.1 %copy-start.8 = (pred[640]{0:T(1024)(128)(4,1)S(1)}, pred[640]{0:T(1024)(128)(4,1)}, u32[]{:S(2)}) copy-start(pred[640]{0:T(1024)(128)(4,1)} %get-tuple-element.163) | copy-start | bytes 1924
  466.3 16.1 %copy-start.9 = (pred[640]{0:T(1024)(128)(4,1)S(1)}, pred[640]{0:T(1024)(128)(4,1)}, u32[]{:S(2)}) copy-start(pred[640]{0:T(1024)(128)(4,1)} %get-tuple-element.164) | copy-start | bytes 1924
  466.3 16.1 %copy-start.10 = (pred[640]{0:T(1024)(128)(4,1)S(1)}, pred[640]{0:T(1024)(128)(4,1)}, u32[]{:S(2)}) copy-start(pred[640]{0:T(1024)(128)(4,1)} %get-tuple-element.165) | copy-start | bytes 1924
  466.3 16.1 %copy-start.11 = (pred[640]{0:T(1024)(128)(4,1)S(1)}, pred[640]{0:T(1024)(128)(4,1)}, u32[]{:S(2)}) copy-start(pred[640]{0:T(1024)(128)(4,1)} %get-tuple-element.166) | copy-start | bytes 1924
  466.3 16.1 %copy-start.12 = (pred[640]{0:T(1024)(128)(4,1)S(1)}, pred[640]{0:T(1024)(128)(4,1)}, u32[]{:S(2)}) copy-start(pred[640]{0:T(1024)(128)(4,1)} %get-tuple-element.167) | copy-start | bytes 1924
  466.3 16.1 %copy-start.13 = (pred[640]{0:T(1024)(128)(4,1)S(1)}, pred[640]{0:T(1024)(128)(4,1)}, u32[]{:S(2)}) copy-start(pred[640]{0:T(1024)(128)(4,1)} %get-tuple-element.168) | copy-start | bytes 1924
  466.3 16.1 %copy-start.14 = (pred[640]{0:T(1024)(128)(4,1)S(1)}, pred[640]{0:T(1024)(128)(4,1)}, u32[]{:S(2)}) copy-start(pred[640]{0:T(1024)(128)(4,1)} %get-tuple-element.169) | copy-start | bytes 1924
  466.3 16.1 %copy-start.15 = (pred[640]{0:T(1024)(128)(4,1)S(1)}, pred[640]{0:T(1024)(128)(4,1)}, u32[]{:S(2)}) copy-start(pred[640]{0:T(1024)(128)(4,1)} %get-tuple-element.170) | copy-start | bytes 1924
  466.3 16.1 %copy-start.16 = (pred[640]{0:T(1024)(128)(4,1)S(1)}, pred[640]{0:T(1024)(128)(4,1)}, u32[]{:S(2)}) copy-start(pred[640]{0:T(1024)(128)(4,1)} %get-tuple-element.171) | copy-start | bytes 1924
  466.3 16.1 %copy-start.17 = (pred[640]{0:T(1024)(128)(4,1)S(1)}, pred[640]{0:T(1024)(128)(4,1)}, u32[]{:S(2)}) copy-start(pred[640]{0:T(1024)(128)(4,1)} %get-tuple-element.172) | copy-start | bytes 1924
  466.3 16.1 %copy-start.18 = (pred[640]{0:T(1024)(128)(4,1)S(1)}, pred[640]{0:T(1024)(128)(4,1)}, u32[]{:S(2)}) copy-start(pred[640]{0:T(1024)(128)(4,1)} %get-tuple-element.173) | copy-start | bytes 1924
  466.4 16.1 %copy-start.19 = (pred[640]{0:T(1024)(128)(4,1)S(1)}, pred[640]{0:T(1024)(128)(4,1)}, u32[]{:S(2)}) copy-start(pred[640]{0:T(1024)(128)(4,1)} %get-tuple-element.174) | copy-start | bytes 1924
  466.4 16.1 %copy-start.20 = (pred[640]{0:T(1024)(128)(4,1)S(1)}, pred[640]{0:T(1024)(128)(4,1)}, u32[]{:S(2)}) copy-start(pred[640]{0:T(1024)(128)(4,1)} %get-tuple-element.175) | copy-start | bytes 1924
  466.4 16.1 %copy-start.21 = (pred[640]{0:T(1024)(128)(4,1)S(1)}, pred[640]{0:T(1024)(128)(4,1)}, u32[]{:S(2)}) copy-start(pred[640]{0:T(1024)(128)(4,1)} %get-tuple-element.176) | copy-start | bytes 1924
  466.4 16.1 %copy-start.22 = (pred[640]{0:T(1024)(128)(4,1)S(1)}, pred[640]{0:T(1024)(128)(4,1)}, u32[]{:S(2)}) copy-start(pred[640]{0:T(1024)(128)(4,1)} %get-tuple-element.177) | copy-start | bytes 1924
  466.4 16.1 %copy-start.23 = (pred[640]{0:T(1024)(128)(4,1)S(1)}, pred[640]{0:T(1024)(128)(4,1)}, u32[]{:S(2)}) copy-start(pred[640]{0:T(1024)(128)(4,1)} %get-tuple-element.178) | copy-start | bytes 1924
  466.4 16.1 %copy-start.24 = (pred[640]{0:T(1024)(128)(4,1)S(1)}, pred[640]{0:T(1024)(128)(4,1)}, u32[]{:S(2)}) copy-start(pred[640]{0:T(1024)(128)(4,1)} %get-tuple-element.179) | copy-start | bytes 1924
  466.4 16.1 %copy-start.25 = (pred[640]{0:T(1024)(128)(4,1)S(1)}, pred[640]{0:T(1024)(128)(4,1)}, u32[]{:S(2)}) copy-start(pred[640]{0:T(1024)(128)(4,1)} %get-tuple-element.180) | copy-start | bytes 1924
  466.4 16.1 %copy-start.26 = (pred[640]{0:T(1024)(128)(4,1)S(1)}, pred[640]{0:T(1024)(128)(4,1)}, u32[]{:S(2)}) copy-start(pred[640]{0:T(1024)(128)(4,1)} %get-tuple-element.181) | copy-start | bytes 1924
  466.4 16.1 %copy-start.27 = (pred[640]{0:T(1024)(128)(4,1)S(1)}, pred[640]{0:T(1024)(128)(4,1)}, u32[]{:S(2)}) copy-start(pred[640]{0:T(1024)(128)(4,1)} %get-tuple-element.182) | copy-start | bytes 1924
  466.4 16.1 %copy-start.28 = (pred[640]{0:T(1024)(128)(4,1)S(1)}, pred[640]{0:T(1024)(128)(4,1)}, u32[]{:S(2)}) copy-start(pred[640]{0:T(1024)(128)(4,1)} %get-tuple-element.183) | copy-start | bytes 1924
  466.5 16.1 %copy-start.29 = (pred[640]{0:T(1024)(128)(4,1)S(1)}, pred[640]{0:T(1024)(128)(4,1)}, u32[]{:S(2)}) copy-start(pred[640]{0:T(1024)(128)(4,1)} %get-tuple-element.184) | copy-start | bytes 1924
  466.5 16.1 %copy-start.30 = (pred[640]{0:T(1024)(128)(4,1)S(1)}, pred[640]{0:T(1024)(128)(4,1)}, u32[]{:S(2)}) copy-start(pred[640]{0:T(1024)(128)(4,1)} %get-tuple-element.185) | copy-start | bytes 1924
  538.0 134.1 %copy-start = (bf16[640,1024]{1,0:T(8,128)(2,1)S(1)}, bf16[640,1024]{1,0:T(8,128)(2,1)}, u32[]{:S(2)}) copy-start(bf16[640,1024]{1,0:T(8,128)(2,1)} %param.7) | copy-start | bytes 3932164
  (20 other events, 241.5 us)
Sparse Core Ops, SparseCore 0:
  9.2 82.4 all-gather.2
  93.4 331.1 all-gather.4
  538.1 133.9 reduce-scatter.1
where the time goes:
time: 682 us; the launch traced here: 681 us
  waiting for transfers between devices  552 us (81%)
  other arithmetic  82.4 us (12%)
  matrix products  21.3 us (3%)
  between operations  15.4 us (2%)
    all_gather x1, waiting for transfers between devices, body(): both_rows = lax.all_gather(both, 'ctx', axis=0, tiled=True)  329 us
    reduce_scatter x1, waiting for transfers between devices, body(): lax.psum_scatter(partial_out.astype(jnp.bfloat16), 'tp', scatter_dimensio...  134 us
    all_gather x1, waiting for transfers between devices, body(): all_feats = lax.all_gather(activations, 'tp', axis=1, tiled=True)  79.5 us
    dot_general x1, other arithmetic, body(): lax.dot_general(gated, out_rows, (((1,), (1,)), ((), ())), preferred_elem...  47.7 us
    add x2, other arithmetic, causal_taps(): summed = summed + jnp.where(in_genome, window * taps[j], jnp.float32(0.0))  23.8 us
    dot_general x1, matrix products, body(): summed = jnp.dot(normed, flat, preferred_element_type=jnp.float32)  13.9 us
  transfers between devices with their start and end apart: 5, of which 5 were waited for; matrix products, arithmetic and copies ran while one was open for 1% of the time, Pallas kernels for 0%

commit v1 on v0

--- a/solution.py
+++ b/solution.py
@@ -43,7 +43,15 @@
         return lax.dynamic_slice_in_dim(source, tail_end - count, count, 0)
 
     gstart = genome_start(positions, genome_starts)
-    all_feats = lax.all_gather(activations, "tp", axis=1, tiled=True)
+    all_feats = jnp.concatenate(
+        lax.all_to_all(
+            jnp.stack(lax.axis_size("tp") * [activations], 0),
+            axis_name="tp",
+            split_axis=0,
+            concat_axis=0,
+        ),
+        axis=1,
+    )
     widened = all_feats.astype(jnp.float32)
     normed = (
         widened * lax.rsqrt(jnp.mean(widened * widened, axis=1, keepdims=True) + 1e-06)

time: 682 us -> 668 us (0.979)
  waiting for transfers between devices: 552 us -> 517 us
  starting transfers between devices: 6.61 us -> 15.7 us
    all_to_all x0 -> x1, waiting for transfers between devices: none -> 167 us  [body(): lax.all_to_all(jnp.stack(lax.axis_size('tp') * [activations], 0), axis_na...]
    all_gather x1, waiting for transfers between devices: 329 us -> 216 us  [body(): both_rows = lax.all_gather(both, 'ctx', axis=0, tiled=True)]
    all_gather x1 -> x0, waiting for transfers between devices: 79.5 us -> none  [body(): all_feats = lax.all_gather(activations, 'tp', axis=1, tiled=True)]
    all_to_all x0 -> x1, starting transfers between devices: none -> 10.1 us  [body(): lax.all_to_all(jnp.stack(lax.axis_size('tp') * [activations], 0), axis_na...]
    reduce_scatter x1, waiting for transfers between devices: 134 us -> 126 us  [body(): lax.psum_scatter(partial_out.astype(jnp.bfloat16), 'tp', scatter_dimensio...]
  transfers between devices with their start and end apart: 5 -> 5, of which waited for: 5 -> 5; matrix products, arithmetic and copies ran while one was open for 1% -> 2% of each run, Pallas kernels for 0% -> 0%
where the time goes in v1:
time: 668 us
  waiting for transfers between devices  517 us (77%)
  other arithmetic  89.2 us (13%)
  matrix products  21.5 us (3%)
  starting transfers between devices  15.7 us (2%)
  between operations  15.6 us (2%)
  local copies, waits for them, and re-layouts  8.96 us (1%)
    all_gather x1, waiting for transfers between devices, body(): both_rows = lax.all_gather(both, 'ctx', axis=0, tiled=True)  216 us
    all_to_all x1, waiting for transfers between devices, body(): lax.all_to_all(jnp.stack(lax.axis_size('tp') * [activations], 0), axis_na...  167 us
    reduce_scatter x1, waiting for transfers between devices, body(): lax.psum_scatter(partial_out.astype(jnp.bfloat16), 'tp', scatter_dimensio...  126 us
    dot_general x1, other arithmetic, body(): lax.dot_general(gated, out_rows, (((1,), (1,)), ((), ())), preferred_elem...  47.7 us
    add x2, other arithmetic, causal_taps(): summed = summed + jnp.where(in_genome, window * taps[j], jnp.float32(0.0))  23.8 us
    dot_general x1, matrix products, body(): summed = jnp.dot(normed, flat, preferred_element_type=jnp.float32)  14 us
  transfers between devices with their start and end apart: 5, of which 5 were waited for; matrix products, arithmetic and copies ran while one was open for 2% of the time, Pallas kernels for 0%

profile of v1, /device:TPU:1, one launch (start us, length us, event | category | flops | bytes accessed | tf_op | source)
XLA Modules:
  0.0 667.9 jit_solution(15426177450977528421)
XLA Ops:
  6.5 0.9 copy.32
  7.5 1.6 pad_maximum_fusion
  9.0 0.0 all-gather.2.cloned.1.call-update
  9.1 1.7 copy.16
  10.8 2.8 stack.2
  13.6 10.1 %all-to-all-start = ((bf16[4,640,1024]{1,2,0:T(8,128)(2,1)}), bf16[4,640,1024]{1,2,0:T(8,128)(2,1)}, u32[]{:S(2)}, u32[]{:S(2)}) async-start(bf16[4,640,1024]{1,2,0:T(8,128)(2,1)} %stack.2), calls=%async_computation | async-start | bytes 10485760 | tf_op jit(solution)/shard_map/all_to_all | solution.py:47
  23.7 0.7 fusion.282
  25.7 0.1 select_reduce_fusion
  26.2 1.3 add_compare_fusion.95
  27.5 166.9 %all-to-all-done = bf16[4,640,1024]{1,2,0:T(8,128)(2,1)} async-done(((bf16[4,640,1024]{1,2,0:T(8,128)(2,1)}), bf16[4,640,1024]{1,2,0:T(8,128)(2,1)}, u32[]{:S(2)}, u32[]{:S(2)}) %all-to-all-start) | async-done | bytes 5242912 | tf_op jit(solution)/shard_map/all_to_all | solution.py:47
  194.4 3.6 multiply_reduce_fusion
  198.0 6.0 fusion.2
  204.0 216.5 %all-gather.2.cloned.1.call-done = bf16[4096,2048]{1,0:T(8,128)(2,1)} async-done(((bf16[64,2048]{1,0:T(8,128)(2,1)}), bf16[4096,2048]{1,0:T(8,128)(2,1)}) %all-gather.2.cloned.1.call-update) | async-done | bytes 16777232 | tf_op jit(solution)/shard_map/all_gather | solution.py:64
  420.4 14.0 %fusion.17 = bf16[640,1536]{1,0:T(8,128)(2,1)} fusion(bf16[640,4096]{0,1:T(8,128)(2,1)} %fusion.2, bf16[4096,2048]{1,0:T(8,128)(2,1)} %all-gather.2.cloned.1.call-done), kind=kOutput, calls=%fused_computation.27 | convolution fusion | flops 8054046720 | bytes 19791872 | tf_op jit(solution)/shard_map/dot_general | solution.py:67
  434.4 2.8 copy.18
  437.2 0.2 constant_dynamic-slice_fusion
  437.4 1.3 collective-permute-start
  438.8 6.2 collective-permute-done
  445.0 1.0 maximum_convert_fusion
  446.0 8.1 %fusion.5 = f32[640,3,512]{0,2,1:T(8,128)S(1)} fusion(f32[646,3,512]{0,2,1:T(8,128)S(1)} %maximum_convert_fusion, f32[3,512]{1,0:T(4,128)S(1)} %get-tuple-element.270, f32[3,512]{1,0:T(4,128)S(1)} %get-tuple-element.271, f32[3,512]{1,0:T(4,128)S(1)} %get-tuple-element.272, f32[3,512]{1,0:T(4,128)S(1)} %get-tuple-element.273, ...), kind=kLoop, calls=%fused_computation.9 | loop fusion | flops 19660800 | bytes 31504768 | tf_op jit(solution)/shard_map/add | solution.py:27
  454.1 0.1 fusion.278
  454.2 0.1 dynamic-slice_bitcast_fusion
  454.3 4.2 collective-permute-start.1
  458.6 0.1 fusion.293
  458.7 1.6 collective-permute-done.1
  460.3 0.4 maximum_convert_fusion.1
  461.1 15.7 %fusion.216 = f32[640,512]{0,1:T(8,128)S(1)} fusion(f32[767,512]{0,1:T(8,128)S(1)} %maximum_convert_fusion.1, f32[512]{0:T(512)S(1)} %bitcast.205, f32[512]{0:T(512)S(1)} %bitcast.187, f32[512]{0:T(512)S(1)} %bitcast.188, f32[512]{0:T(512)S(1)} %bitcast.189, f32[512]{0:T(512)S(1)} %bitcast.190, f32[512]{0:T(512)S(1)} %bitcast.191, f32[512]{0:T(512)S(1)} %bitcast.192, ...), kind=kLoop, calls=%fused_computation.323 | loop fusion | flops 31129600 | bytes 43339776 | tf_op jit(solution)/shard_map/add | solution.py:27
  477.2 47.7 %fusion.300 = bf16[640,512]{0,1:T(8,128)(2,1)S(1)} fusion(f32[767,512]{0,1:T(8,128)S(1)} %maximum_convert_fusion.1, f32[640,512]{0,1:T(8,128)S(1)} %fusion.216, f32[512]{0:T(512)S(1)} %bitcast.206, f32[512]{0:T(512)S(1)} %bitcast.207, f32[512]{0:T(512)S(1)} %bitcast.246, f32[512]{0:T(512)S(1)} %bitcast.247, f32[512]{0:T(512)S(1)} %bitcast.248, ...), kind=kLoop, calls=%fused_computation.35.clone.clone.2 | loop fusion | flops 95027200 | bytes 129363968 | tf_op jit(solution)/shard_map/dot_general | solution.py:87
  524.9 7.5 %convolution_convert_fusion = bf16[640,4096]{1,0:T(8,128)(2,1)} fusion(bf16[4096,2048]{1,0:T(8,128)(2,1)} %all-gather.2.cloned.1.call-done, bf16[640,512]{0,1:T(8,128)(2,1)S(1)} %fusion.300), kind=kOutput, calls=%fused_computation.5 | convolution fusion | flops 2686976000 | bytes 10092544 | tf_op jit(solution)/shard_map/dot_general | solution.py:87
  532.4 0.0 reduce-scatter.2.cloned.1.call-update
  532.5 125.8 %reduce-scatter.2.cloned.1.call-done = bf16[640,1024]{1,0:T(8,128)(2,1)} async-done(((bf16[640,4096]{1,0:T(8,128)(2,1)}), bf16[640,1024]{1,0:T(8,128)(2,1)}) %reduce-scatter.2.cloned.1.call-update) | async-done | bytes 1310736 | tf_op jit(solution)/shard_map/reduce_scatter | solution.py:90
  658.3 2.8 fusion.20
  (107 shorter events, 0.5 us)
Async XLA Ops:
  6.5 413.9 %all-gather.2.cloned.1.call-start = ((), (), s32[]{:S(2)}) async-start(), calls=%async_computation.2 | async-start | bytes 17039360 | tf_op jit(solution)/shard_map/all_gather | solution.py:64
  13.6 180.8 %all-to-all-start = ((bf16[4,640,1024]{1,2,0:T(8,128)(2,1)}), bf16[4,640,1024]{1,2,0:T(8,128)(2,1)}, u32[]{:S(2)}, u32[]{:S(2)}) async-start(bf16[4,640,1024]{1,2,0:T(8,128)(2,1)} %stack.2), calls=%async_computation | async-start | bytes 10485760 | tf_op jit(solution)/shard_map/all_to_all | solution.py:47
  23.7 634.6 %reduce-scatter.2.cloned.1.call-start = ((), (), s32[]{:S(2)}) async-start(), calls=%async_computation.3 | async-start | bytes 6553600 | tf_op jit(solution)/shard_map/reduce_scatter | solution.py:90
  437.4 7.5 %collective-permute-start = (bf16[6,3,512]{0,2,1:T(8,128)(2,1)S(1)}, bf16[6,3,512]{0,2,1:T(8,128)(2,1)S(1)}, u32[]{:S(2)}, u32[]{:S(2)}) collective-permute-start(bf16[6,3,512]{0,2,1:T(8,128)(2,1)S(1)} %constant_dynamic-slice_fusion), channel_id=1, source_target_pairs={{0,4},{4,8},{8,12},{12,16},{16,20},{20,24},{24,28},{28,32},{32,36}... | collective-permute-start | bytes 55304 | tf_op jit(solution)/shard_map/ppermute | solution.py:12
  454.3 6.0 collective-permute-start.1
  460.7 16.1 %copy-start.3 = (pred[640]{0:T(1024)(128)(4,1)S(1)}, pred[640]{0:T(1024)(128)(4,1)}, u32[]{:S(2)}) copy-start(pred[640]{0:T(1024)(128)(4,1)} %get-tuple-element.160) | copy-start | bytes 1924
  460.7 16.1 %copy-start.4 = (pred[640]{0:T(1024)(128)(4,1)S(1)}, pred[640]{0:T(1024)(128)(4,1)}, u32[]{:S(2)}) copy-start(pred[640]{0:T(1024)(128)(4,1)} %get-tuple-element.161) | copy-start | bytes 1924
  460.7 16.1 %copy-start.5 = (pred[640]{0:T(1024)(128)(4,1)S(1)}, pred[640]{0:T(1024)(128)(4,1)}, u32[]{:S(2)}) copy-start(pred[640]{0:T(1024)(128)(4,1)} %get-tuple-element.162) | copy-start | bytes 1924
  460.7 16.1 %copy-start.6 = (pred[640]{0:T(1024)(128)(4,1)S(1)}, pred[640]{0:T(1024)(128)(4,1)}, u32[]{:S(2)}) copy-start(pred[640]{0:T(1024)(128)(4,1)} %get-tuple-element.163) | copy-start | bytes 1924
  460.7 16.1 %copy-start.7 = (pred[640]{0:T(1024)(128)(4,1)S(1)}, pred[640]{0:T(1024)(128)(4,1)}, u32[]{:S(2)}) copy-start(pred[640]{0:T(1024)(128)(4,1)} %get-tuple-element.164) | copy-start | bytes 1924
  460.7 16.1 %copy-start.8 = (pred[640]{0:T(1024)(128)(4,1)S(1)}, pred[640]{0:T(1024)(128)(4,1)}, u32[]{:S(2)}) copy-start(pred[640]{0:T(1024)(128)(4,1)} %get-tuple-element.165) | copy-start | bytes 1924
  460.7 16.1 %copy-start.9 = (pred[640]{0:T(1024)(128)(4,1)S(1)}, pred[640]{0:T(1024)(128)(4,1)}, u32[]{:S(2)}) copy-start(pred[640]{0:T(1024)(128)(4,1)} %get-tuple-element.166) | copy-start | bytes 1924
  460.8 16.1 %copy-start.10 = (pred[640]{0:T(1024)(128)(4,1)S(1)}, pred[640]{0:T(1024)(128)(4,1)}, u32[]{:S(2)}) copy-start(pred[640]{0:T(1024)(128)(4,1)} %get-tuple-element.167) | copy-start | bytes 1924
  460.8 16.1 %copy-start.11 = (pred[640]{0:T(1024)(128)(4,1)S(1)}, pred[640]{0:T(1024)(128)(4,1)}, u32[]{:S(2)}) copy-start(pred[640]{0:T(1024)(128)(4,1)} %get-tuple-element.168) | copy-start | bytes 1924
  460.8 16.1 %copy-start.12 = (pred[640]{0:T(1024)(128)(4,1)S(1)}, pred[640]{0:T(1024)(128)(4,1)}, u32[]{:S(2)}) copy-start(pred[640]{0:T(1024)(128)(4,1)} %get-tuple-element.169) | copy-start | bytes 1924
  460.8 16.1 %copy-start.13 = (pred[640]{0:T(1024)(128)(4,1)S(1)}, pred[640]{0:T(1024)(128)(4,1)}, u32[]{:S(2)}) copy-start(pred[640]{0:T(1024)(128)(4,1)} %get-tuple-element.170) | copy-start | bytes 1924
  460.8 16.1 %copy-start.14 = (pred[640]{0:T(1024)(128)(4,1)S(1)}, pred[640]{0:T(1024)(128)(4,1)}, u32[]{:S(2)}) copy-start(pred[640]{0:T(1024)(128)(4,1)} %get-tuple-element.171) | copy-start | bytes 1924
  460.8 16.1 %copy-start.15 = (pred[640]{0:T(1024)(128)(4,1)S(1)}, pred[640]{0:T(1024)(128)(4,1)}, u32[]{:S(2)}) copy-start(pred[640]{0:T(1024)(128)(4,1)} %get-tuple-element.172) | copy-start | bytes 1924
  460.8 16.1 %copy-start.16 = (pred[640]{0:T(1024)(128)(4,1)S(1)}, pred[640]{0:T(1024)(128)(4,1)}, u32[]{:S(2)}) copy-start(pred[640]{0:T(1024)(128)(4,1)} %get-tuple-element.173) | copy-start | bytes 1924
  460.8 16.1 %copy-start.17 = (pred[640]{0:T(1024)(128)(4,1)S(1)}, pred[640]{0:T(1024)(128)(4,1)}, u32[]{:S(2)}) copy-start(pred[640]{0:T(1024)(128)(4,1)} %get-tuple-element.174) | copy-start | bytes 1924
  460.8 16.1 %copy-start.18 = (pred[640]{0:T(1024)(128)(4,1)S(1)}, pred[640]{0:T(1024)(128)(4,1)}, u32[]{:S(2)}) copy-start(pred[640]{0:T(1024)(128)(4,1)} %get-tuple-element.175) | copy-start | bytes 1924
  460.8 16.1 %copy-start.19 = (pred[640]{0:T(1024)(128)(4,1)S(1)}, pred[640]{0:T(1024)(128)(4,1)}, u32[]{:S(2)}) copy-start(pred[640]{0:T(1024)(128)(4,1)} %get-tuple-element.176) | copy-start | bytes 1924
  460.9 16.1 %copy-start.20 = (pred[640]{0:T(1024)(128)(4,1)S(1)}, pred[640]{0:T(1024)(128)(4,1)}, u32[]{:S(2)}) copy-start(pred[640]{0:T(1024)(128)(4,1)} %get-tuple-element.177) | copy-start | bytes 1924
  460.9 16.1 %copy-start.21 = (pred[640]{0:T(1024)(128)(4,1)S(1)}, pred[640]{0:T(1024)(128)(4,1)}, u32[]{:S(2)}) copy-start(pred[640]{0:T(1024)(128)(4,1)} %get-tuple-element.178) | copy-start | bytes 1924
  460.9 16.1 %copy-start.22 = (pred[640]{0:T(1024)(128)(4,1)S(1)}, pred[640]{0:T(1024)(128)(4,1)}, u32[]{:S(2)}) copy-start(pred[640]{0:T(1024)(128)(4,1)} %get-tuple-element.179) | copy-start | bytes 1924
  460.9 16.1 %copy-start.23 = (pred[640]{0:T(1024)(128)(4,1)S(1)}, pred[640]{0:T(1024)(128)(4,1)}, u32[]{:S(2)}) copy-start(pred[640]{0:T(1024)(128)(4,1)} %get-tuple-element.180) | copy-start | bytes 1924
  460.9 16.1 %copy-start.24 = (pred[640]{0:T(1024)(128)(4,1)S(1)}, pred[640]{0:T(1024)(128)(4,1)}, u32[]{:S(2)}) copy-start(pred[640]{0:T(1024)(128)(4,1)} %get-tuple-element.181) | copy-start | bytes 1924
  460.9 16.1 %copy-start.25 = (pred[640]{0:T(1024)(128)(4,1)S(1)}, pred[640]{0:T(1024)(128)(4,1)}, u32[]{:S(2)}) copy-start(pred[640]{0:T(1024)(128)(4,1)} %get-tuple-element.182) | copy-start | bytes 1924
  460.9 16.1 %copy-start.26 = (pred[640]{0:T(1024)(128)(4,1)S(1)}, pred[640]{0:T(1024)(128)(4,1)}, u32[]{:S(2)}) copy-start(pred[640]{0:T(1024)(128)(4,1)} %get-tuple-element.183) | copy-start | bytes 1924
  460.9 16.1 %copy-start.27 = (pred[640]{0:T(1024)(128)(4,1)S(1)}, pred[640]{0:T(1024)(128)(4,1)}, u32[]{:S(2)}) copy-start(pred[640]{0:T(1024)(128)(4,1)} %get-tuple-element.184) | copy-start | bytes 1924
  460.9 16.1 %copy-start.28 = (pred[640]{0:T(1024)(128)(4,1)S(1)}, pred[640]{0:T(1024)(128)(4,1)}, u32[]{:S(2)}) copy-start(pred[640]{0:T(1024)(128)(4,1)} %get-tuple-element.185) | copy-start | bytes 1924
  532.4 125.8 %copy-start = (bf16[640,1024]{1,0:T(8,128)(2,1)S(1)}, bf16[640,1024]{1,0:T(8,128)(2,1)}, u32[]{:S(2)}) copy-start(bf16[640,1024]{1,0:T(8,128)(2,1)} %param.7) | copy-start | bytes 3932164
  (18 other events, 272.8 us)
Sparse Core Ops, SparseCore 0:
  9.2 411.1 all-gather.1
  532.6 125.6 reduce-scatter.1
